TPU v7x, 256 devices: a whole 4x4x8 slice. The times are simulated.
256 devices in a mesh: cfg: 2 (over z_lo), req: 16 (over y, z_hi), mlp: 8 (over x, core).
Axes of the slice: x: 4, y: 4, z: 8 (z_hi: 4, z_lo: 2; z = z_hi * 2 + z_lo), core: 2. Of those that a mesh axis runs over, the one named last changes fastest.
Arguments:
- hidden: bfloat16 [2, 16384, 1152], P('cfg', ('req', 'mlp')), may hold values from -64 to 64
- noisy_latent: float32 [16384, 16], P(('req', 'mlp'), 'cfg'), may hold values from -6 to 6
- labels: int32 [16, 4], replicated, may hold values from 0 to 999
- timesteps: int32 [16, 4], replicated, may hold values from 0 to 999
- lengths: int32 [16, 4], P('req'), may hold values from 1 to 512, 1024 in all within a row
- guidance: float32 [16, 4], P('req'), may hold values from 1.5 to 4
- keep_scale: float32 [16, 4], P('req'), may hold values from 0.9 to 1.2
- noise_scale: float32 [16, 4], P('req'), may hold values from -0.8 to -0.2
- class_table: bfloat16 [1001, 1152], replicated, may hold values from -6 to 6
- time_up: bfloat16 [256, 1152], replicated, may hold values from -0.375 to 0.375
- time_up_bias: bfloat16 [1152], replicated, may hold values from -4 to 4
- time_out: bfloat16 [1152, 1152], replicated, may hold values from -0.1875 to 0.1875
- time_out_bias: bfloat16 [1152], replicated, may hold values from -4 to 4
- mod_weight: bfloat16 [1152, 9216], P(None, 'req'), may hold values from -0.1875 to 0.1875
- mod_bias: bfloat16 [9216], P('req'), may hold values from -4 to 4
- qkv_weight: bfloat16 [1152, 3456], P(None, 'req'), may hold values from -8 to 8
- qkv_bias: bfloat16 [3456], P('req'), may hold values from -4 to 4
- out_weight: bfloat16 [1152, 1152], P(None, 'req'), may hold values from -0.1875 to 0.1875
- out_bias: bfloat16 [1152], P('req'), may hold values from -4 to 4
- up_weight: bfloat16 [1152, 4608], P(None, 'mlp'), may hold values from -0.1875 to 0.1875
- up_bias: bfloat16 [4608], P('mlp'), may hold values from -4 to 4
- down_weight: bfloat16 [4608, 1152], P('mlp'), may hold values from -1 to 1
- down_bias: bfloat16 [1152], replicated, may hold values from -4 to 4
- final_weight: bfloat16 [1152, 16], replicated, may hold values from -0.1875 to 0.1875
- final_bias: bfloat16 [16], replicated, may hold values from -4 to 4
Outputs:
- next_latent: float32 [16384, 16], P(('req', 'mlp'), 'cfg')
Inputs may be any that keep to these rules, and one draw needn't show every extreme that they name: `lengths`: each row sums to 1024, and its largest crop has exactly 512 tokens.
All inputs are finite; a program needn't handle non-finite values.
Results may differ from a plain program's by a relative error of at most 0.015.
Values may be sent and summed in bfloat16 or wider, within the bound.
No kernel may reach another device: no remote copies, remote signals or barrier semaphores. Data moves between devices by JAX's collectives and lax.ppermute only.
A program may use at most 128 MiB of HBM per device.

v0:
```python
import math
import jax
import jax.numpy as jnp
from jax import lax
from jax.sharding import PartitionSpec as P

HEADS = 16
HEAD_DIM = 72
CLASSES = 1000
FREQ = 256


def layer_norm(values):
    values = values.astype(jnp.float32)
    centre = values - jnp.mean(values, axis=-1, keepdims=True)
    variance = jnp.mean(centre * centre, axis=-1, keepdims=True)
    return centre * lax.rsqrt(variance + 1e-06)


def time_features(times_flat):
    half_freq = FREQ // 2
    frequency = jnp.exp(-math.log(10000.0) * jnp.arange(half_freq, dtype=jnp.float32) / half_freq)
    angles = times_flat.astype(jnp.float32)[:, None] * frequency[None, :]
    return jnp.concatenate([jnp.cos(angles), jnp.sin(angles)], axis=1).astype(jnp.bfloat16)


def segment_ids(lengths_row, positions):
    ends = jnp.cumsum(lengths_row)
    return jnp.sum((positions[:, None] >= ends[None, :]).astype(jnp.int32), axis=1)


def attention(queries, keys_all, values_all, query_segment, key_segment):
    scores = jnp.einsum(
        "qhd,khd->hqk", queries, keys_all, preferred_element_type=jnp.float32
    ) / math.sqrt(HEAD_DIM)
    same = (query_segment[:, None] == key_segment[None, :])[None]
    masked = jnp.where(same, scores, -1e30)
    row_max = jnp.max(masked, axis=2, keepdims=True)
    expo = jnp.where(same, jnp.exp(masked - row_max), 0.0)
    denominator = jnp.sum(expo, axis=2)
    weights = expo.astype(jnp.bfloat16)
    mixed = jnp.einsum("hqk,khd->qhd", weights, values_all, preferred_element_type=jnp.float32)
    result = mixed / jnp.transpose(denominator)[:, :, None]
    return result.astype(jnp.bfloat16).reshape(queries.shape[0], -1)


def shards(
    hidden,
    noisy_latent,
    labels,
    timesteps,
    lengths,
    guidance,
    keep_scale,
    noise_scale,
    class_table,
    time_up,
    time_up_bias,
    time_out,
    time_out_bias,
    mod_weight,
    mod_bias,
    qkv_weight,
    qkv_bias,
    out_weight,
    out_bias,
    up_weight,
    up_bias,
    down_weight,
    down_bias,
    final_weight,
    final_bias,
):
    req_count = lax.axis_size("req")
    mlp_count = lax.axis_size("mlp")
    half_index = lax.axis_index("cfg")
    mlp_index = lax.axis_index("mlp")
    tok_rows = hidden.shape[1]
    width = hidden.shape[2]
    group_rows = tok_rows * mlp_count
    per_group = labels.shape[1]
    time_feat = time_features(timesteps.reshape(-1))
    time_mid = jax.nn.silu(
        jnp.dot(time_feat, time_up, preferred_element_type=jnp.float32)
        + time_up_bias.astype(jnp.float32)
    ).astype(jnp.bfloat16)
    time_cond = jnp.dot(
        time_mid, time_out, preferred_element_type=jnp.float32
    ) + time_out_bias.astype(jnp.float32)
    used_labels = jnp.where(half_index == 0, labels.reshape(-1), CLASSES)
    one_hot = (used_labels[:, None] == jnp.arange(CLASSES + 1, dtype=jnp.int32)[None, :]).astype(
        jnp.bfloat16
    )
    cond_act = jax.nn.silu(
        time_cond + jnp.dot(one_hot, class_table, preferred_element_type=jnp.float32)
    ).astype(jnp.bfloat16)
    local_mod = (
        jnp.dot(cond_act, mod_weight, preferred_element_type=jnp.float32)
        + mod_bias.astype(jnp.float32)
    ).astype(jnp.bfloat16)
    local_mod = local_mod.reshape(req_count, per_group, local_mod.shape[1])
    modulation = lax.all_to_all(local_mod, "req", split_axis=0, concat_axis=2, tiled=True)[0]
    positions = jnp.arange(group_rows, dtype=jnp.int32)
    segment_all = segment_ids(lengths[0], positions)
    segment_own = lax.dynamic_slice_in_dim(segment_all, mlp_index * tok_rows, tok_rows)
    member = segment_own[:, None] == jnp.arange(per_group, dtype=jnp.int32)[None, :]
    per_token = jnp.dot(member.astype(jnp.bfloat16), modulation, preferred_element_type=jnp.float32)
    pieces = [per_token[:, index * width : (index + 1) * width] for index in range(8)]
    shift_attn, scale_attn, gate_attn, shift_mlp, scale_mlp, gate_mlp, shift_final, scale_final = (
        pieces
    )
    rows = hidden[0]
    normed = (layer_norm(rows) * (1.0 + scale_attn) + shift_attn).astype(jnp.bfloat16)
    core = mlp_index % 2
    half_rows = width // 2
    pair = [(index, index ^ 1) for index in range(mlp_count)]

    def split_gather(weight, bias):
        mine = lax.dynamic_slice_in_dim(weight, core * half_rows, half_rows, axis=0)
        bias_rows = jnp.zeros((16, weight.shape[1]), weight.dtype).at[0].set(bias)
        gathered = lax.all_gather(
            jnp.concatenate([mine, bias_rows], axis=0), "req", axis=1, tiled=True
        )
        return (gathered, lax.ppermute(gathered, "mlp", pair))

    def split_dot(values, mine, other):
        values_mine = lax.dynamic_slice_in_dim(values, core * half_rows, half_rows, axis=1)
        values_other = lax.dynamic_slice_in_dim(values, (1 - core) * half_rows, half_rows, axis=1)
        return (
            jnp.dot(values_mine, mine[:half_rows], preferred_element_type=jnp.float32)
            + jnp.dot(values_other, other[:half_rows], preferred_element_type=jnp.float32)
            + mine[half_rows].astype(jnp.float32)
        )

    qkv_mine, qkv_other = split_gather(qkv_weight, qkv_bias)
    out_mine, out_other = split_gather(out_weight, out_bias)
    qkv = split_dot(normed, qkv_mine, qkv_other).astype(jnp.bfloat16)
    heads_per = HEADS // mlp_count
    head_cols = heads_per * HEAD_DIM
    packed = jnp.transpose(qkv.reshape(tok_rows, 3, mlp_count, head_cols), (0, 2, 1, 3)).reshape(
        tok_rows, mlp_count * 3 * head_cols
    )
    own_heads = lax.all_to_all(packed, "mlp", split_axis=1, concat_axis=0, tiled=True)
    attended_heads = attention(
        own_heads[:, :head_cols].reshape(group_rows, heads_per, HEAD_DIM),
        own_heads[:, head_cols : 2 * head_cols].reshape(group_rows, heads_per, HEAD_DIM),
        own_heads[:, 2 * head_cols :].reshape(group_rows, heads_per, HEAD_DIM),
        segment_all,
        segment_all,
    )
    attended = lax.all_to_all(attended_heads, "mlp", split_axis=0, concat_axis=1, tiled=True)
    projected = split_dot(attended, out_mine, out_other)
    mid_hidden = (rows.astype(jnp.float32) + gate_attn * projected).astype(jnp.bfloat16)
    normed_mlp = (layer_norm(mid_hidden) * (1.0 + scale_mlp) + shift_mlp).astype(jnp.bfloat16)
    gathered = lax.all_gather(normed_mlp, "mlp", axis=0, tiled=True)
    inner = jax.nn.gelu(
        jnp.dot(gathered, up_weight, preferred_element_type=jnp.float32)
        + up_bias.astype(jnp.float32),
        approximate=True,
    ).astype(jnp.bfloat16)
    mlp_out = lax.psum_scatter(
        jnp.dot(inner, down_weight, preferred_element_type=jnp.float32).astype(jnp.bfloat16),
        "mlp",
        scatter_dimension=0,
        tiled=True,
    ).astype(jnp.float32)
    final_hidden = mid_hidden.astype(jnp.float32) + gate_mlp * (
        mlp_out + down_bias.astype(jnp.float32)
    )
    normed_final = (layer_norm(final_hidden) * (1.0 + scale_final) + shift_final).astype(
        jnp.bfloat16
    )
    predicted = jnp.dot(
        normed_final, final_weight, preferred_element_type=jnp.float32
    ) + final_bias.astype(jnp.float32)
    halves = lax.all_to_all(predicted[None], "cfg", split_axis=2, concat_axis=0, tiled=True)
    eps_cond = halves[0]
    eps_free = halves[1]
    member_f = member.astype(jnp.float32)
    guide_tok = jnp.sum(member_f * guidance, axis=1, keepdims=True)
    keep_tok = jnp.sum(member_f * keep_scale, axis=1, keepdims=True)
    noise_tok = jnp.sum(member_f * noise_scale, axis=1, keepdims=True)
    return keep_tok * noisy_latent + noise_tok * (eps_free + guide_tok * (eps_cond - eps_free))


def solution(mesh):
    return jax.shard_map(
        shards,
        mesh=mesh,
        in_specs=(
            P("cfg", ("req", "mlp"), None),
            P(("req", "mlp"), "cfg"),
            P(),
            P(),
            P("req", None),
            P("req", None),
            P("req", None),
            P("req", None),
            P(),
            P(),
            P(),
            P(),
            P(),
            P(None, "req"),
            P("req"),
            P(None, "req"),
            P("req"),
            P(None, "req"),
            P("req"),
            P(None, "mlp"),
            P("mlp"),
            P("mlp", None),
            P(),
            P(),
            P(),
        ),
        out_specs=P(("req", "mlp"), "cfg"),
        check_vma=False,
    )
```

profile of v0, /device:TPU:8, one launch (start us, length us, event | category | flops | bytes accessed | tf_op | source)
XLA Modules:
  0.0 295.6 jit_solution(11914430172864486977)
XLA Ops:
  9.5 79.9 %all-gather.4.cloned.1.call-done = bf16[592,3456]{0,1:T(8,128)(2,1)} async-done(((bf16[592,216]{0,1:T(8,128)(2,1)}), bf16[592,3456]{0,1:T(8,128)(2,1)}) %all-gather.4.cloned.1.call-update) | async-done | bytes 4091920 | tf_op jit(solution)/shard_map/all_gather | solution.py:121
  89.3 7.0 %copy.82 = bf16[592,3456]{1,0:T(8,128)(2,1)} copy(bf16[592,3456]{0,1:T(8,128)(2,1)} %all-gather.4.cloned.1.call-done) | data formatting | bytes 8183808 | tf_op jit(solution)/shard_map/all_gather | solution.py:121
  97.0 1.8 convolution_add_fusion.3
  98.9 3.0 %fusion.37 = bf16[64,576]{1,0:T(8,128)(2,1)S(1)} fusion(bf16[1152,576]{0,1:T(8,128)(2,1)} %param.42, f32[64,1152]{1,0:T(8,128)S(1)} %convolution_add_fusion.3, bf16[1001,1152]{1,0:T(8,128)(2,1)} %param.37, s32[64]{0:T(128)S(1)} %select_n.45, f32[576]{0:T(1024)S(1)} %convert_element_type.98), kind=kOutput, calls=%fused_computation.43 | convolution fusion | flops 233118272 | bytes 4004608 | tf_op jit(solution)/shard_map/dot_general | solution.py:98
  102.6 9.5 %all-to-all-start = ((bf16[16,4,576]{2,1,0:T(4,128)(2,1)}), bf16[16,4,576]{2,1,0:T(4,128)(2,1)S(1)}, u32[]{:S(2)}, u32[]{:S(2)}) async-start(bf16[16,4,576]{2,1,0:T(4,128)(2,1)} %reshape.206), calls=%async_computation | async-start | bytes 163840 | tf_op jit(solution)/shard_map/all_to_all | solution.py:102
  113.8 6.9 %all-to-all-done = bf16[16,4,576]{2,1,0:T(4,128)(2,1)S(1)} async-done(((bf16[16,4,576]{2,1,0:T(4,128)(2,1)}), bf16[16,4,576]{2,1,0:T(4,128)(2,1)S(1)}, u32[]{:S(2)}, u32[]{:S(2)}) %all-to-all-start) | async-done | bytes 73760 | tf_op jit(solution)/shard_map/all_to_all | solution.py:102
  121.8 2.1 copy-done.1
  124.1 1.8 convert_reduce_fusion
  125.9 3.7 %fusion.4 = f32[128,3456]{1,0:T(8,128)S(1)} fusion(bf16[592,3456]{0,1:T(8,128)(2,1)} %all-gather.4.cloned.1.call-done, bf16[128,1152]{1,0:T(8,128)(2,1)S(1)} %fusion.46, s32[]{:T(128)S(6)} %select_n.47), kind=kOutput, calls=%fused_computation.7 | convolution fusion | flops 509607936 | bytes 6025220 | tf_op jit(solution)/shard_map/dot_general | solution.py:130
  129.7 4.0 %fusion.3 = bf16[128,3456]{1,0:T(8,128)(2,1)} fusion(f32[128,3456]{1,0:T(8,128)S(1)} %fusion.4, bf16[592,3456]{1,0:T(8,128)(2,1)} %collective-permute-done, f32[3456]{0:T(1024)S(1)} %convert_reduce_fusion, bf16[128,1152]{1,0:T(8,128)(2,1)S(1)} %fusion.46, s32[]{:T(128)S(6)} %select_n.48), kind=kOutput, calls=%fused_computation.6 | convolution fusion | flops 510935040 | bytes 6815748 | tf_op jit(solution)/shard_map/dot_general | solution.py:131
  133.7 2.2 copy.83
  136.0 2.2 copy.84
  138.1 4.2 %all-to-all-start.1 = ((bf16[128,8,432]{0,2,1:T(8,128)(2,1)}), bf16[128,8,432]{0,2,1:T(8,128)(2,1)}, u32[]{:S(2)}, u32[]{:S(2)}) async-start(bf16[128,8,432]{0,2,1:T(8,128)(2,1)} %bitcast.96), calls=%async_computation.1 | async-start | bytes 1769472 | tf_op jit(solution)/shard_map/all_to_all | solution.py:143
  142.4 1.6 broadcast_compare_fusion
  144.0 26.4 %all-gather.6.cloned.1.call-done = bf16[592,1152]{0,1:T(8,128)(2,1)} async-done(((bf16[592,72]{0,1:T(8,128)(2,1)}), bf16[592,1152]{0,1:T(8,128)(2,1)}) %all-gather.6.cloned.1.call-update) | async-done | bytes 1363984 | tf_op jit(solution)/shard_map/all_gather | solution.py:121
  170.4 3.6 %copy.89 = bf16[592,1152]{1,0:T(8,128)(2,1)} copy(bf16[592,1152]{0,1:T(8,128)(2,1)} %all-gather.6.cloned.1.call-done) | data formatting | bytes 2727936 | tf_op jit(solution)/shard_map/all_gather | solution.py:121
  174.0 1.3 copy_bitcast_fusion
  176.1 8.4 %fusion.99 = (f32[2,1024]{1,0:T(2,128)S(1)}, bf16[2,1024,1024]{1,2,0:T(8,128)(2,1)}) fusion(pred[1024,1024]{0,1:T(8,128)(4,1)} %broadcast_compare_fusion, bf16[1024,2,72]{0,2,1:T(8,128)(2,1)} %bitcast.104, bf16[1024,2,72]{0,2,1:T(8,128)(2,1)S(1)} %bitcast.103), kind=kOutput, calls=%fused_computation.135 | convolution fusion | flops 314573824 | bytes 5840896 | tf_op jit(solution)/shard_map/sub | solution.py:39
  184.5 3.0 %fusion.34 = bf16[1024,2,72]{0,2,1:T(8,128)(2,1)S(1)} fusion(bf16[1024,2,72]{0,2,1:T(8,128)(2,1)S(1)} %bitcast.102, bf16[2,1024,1024]{1,2,0:T(8,128)(2,1)} %get-tuple-element.40, f32[1024,2]{0,1:T(2,128)S(1)} %bitcast.113), kind=kOutput, calls=%fused_computation.41 | convolution fusion | flops 302284800 | bytes 4792320 | tf_op jit(solution)/shard_map/hqk,khd->qhd/dot_general | solution.py:42
  188.3 4.2 %all-to-all-start.2 = ((bf16[8,128,144]{1,2,0:T(8,128)(2,1)}), bf16[8,128,144]{1,2,0:T(8,128)(2,1)S(1)}, u32[]{:S(2)}, u32[]{:S(2)}) async-start(bf16[8,128,144]{1,2,0:T(8,128)(2,1)} %copy.87), calls=%async_computation.2 | async-start | bytes 589824 | tf_op jit(solution)/shard_map/all_to_all | solution.py:151
  192.6 1.2 convert_reduce_fusion.2
  193.8 6.6 %all-to-all-done.2 = bf16[8,128,144]{1,2,0:T(8,128)(2,1)S(1)} async-done(((bf16[8,128,144]{1,2,0:T(8,128)(2,1)}), bf16[8,128,144]{1,2,0:T(8,128)(2,1)S(1)}, u32[]{:S(2)}, u32[]{:S(2)}) %all-to-all-start.2) | async-done | bytes 294944 | tf_op jit(solution)/shard_map/all_to_all | solution.py:151
  200.4 2.1 fusion.25
  202.5 2.1 fusion.100
  204.8 2.2 fusion.49
  207.1 25.0 %all-gather.8.cloned.1.call-done = bf16[1024,1152]{1,0:T(8,128)(2,1)} async-done(((bf16[128,1152]{1,0:T(8,128)(2,1)}), bf16[1024,1152]{1,0:T(8,128)(2,1)}) %all-gather.8.cloned.1.call-update) | async-done | bytes 2359312 | tf_op jit(solution)/shard_map/all_gather | solution.py:155
  232.1 7.9 %convolution_convert_fusion = bf16[1024,1152]{1,0:T(8,128)(2,1)} fusion(bf16[576,1152]{1,0:T(8,128)(2,1)} %param.50, bf16[1024,1152]{1,0:T(8,128)(2,1)} %all-gather.8.cloned.1.call-done, bf16[1152,576]{0,1:T(8,128)(2,1)} %param.48, f32[576]{0:T(1024)S(1)} %convert_element_type.107), kind=kOutput, calls=%fused_computation.15 | convolution fusion | flops 2724986880 | bytes 7375104 | tf_op jit(solution)/shard_map/dot_general | solution.py:162
  240.7 37.0 %reduce-scatter.2.cloned.1.call-done = bf16[128,1152]{1,0:T(8,128)(2,1)} async-done(((bf16[1024,1152]{1,0:T(8,128)(2,1)}), bf16[128,1152]{1,0:T(8,128)(2,1)}) %reduce-scatter.2.cloned.1.call-update) | async-done | bytes 294928 | tf_op jit(solution)/shard_map/reduce_scatter | solution.py:161
  277.7 1.3 fusion.96
  279.3 2.2 convolution_add_fusion.6
  281.4 3.2 %all-to-all-start.3 = ((f32[1,128,16]{1,0,2:T(1,128)}), f32[1,128,16]{1,0,2:T(1,128)S(1)}, u32[]{:S(2)}, u32[]{:S(2)}) async-start(f32[1,128,16]{1,0,2:T(1,128)} %bitcast.21), calls=%async_computation.4 | async-start | bytes 16384 | tf_op jit(solution)/shard_map/all_to_all | solution.py:176
  284.8 3.7 %all-to-all-done.3 = f32[1,128,16]{1,0,2:T(1,128)S(1)} async-done(((f32[1,128,16]{1,0,2:T(1,128)}), f32[1,128,16]{1,0,2:T(1,128)S(1)}, u32[]{:S(2)}, u32[]{:S(2)}) %all-to-all-start.3) | async-done | bytes 8224 | tf_op jit(solution)/shard_map/all_to_all | solution.py:176
  (95 shorter events, 10.6 us)
Async XLA Ops:
  6.5 90.5 %copy-start = (bf16[1152,1152]{1,0:T(8,128)(2,1)S(1)}, bf16[1152,1152]{1,0:T(8,128)(2,1)}, u32[]{:S(2)}) copy-start(bf16[1152,1152]{1,0:T(8,128)(2,1)} %param.40) | copy-start | bytes 7962628
  6.5 82.8 %all-gather.4.cloned.1.call-start = ((), (), s32[]{:S(2)}) async-start(), calls=%async_computation.5 | async-start | bytes 4700160 | tf_op jit(solution)/shard_map/all_gather | solution.py:121
  9.4 87.0 %copy-start.12 = (s32[16,4]{0,1:T(4,128)S(1)}, s32[16,4]{0,1:T(4,128)}, u32[]{:S(2)}) copy-start(s32[16,4]{0,1:T(4,128)} %param.32) | copy-start | bytes 772
  9.4 87.1 %copy-start.6 = (bf16[1152]{0:T(1024)(128)(2,1)S(1)}, bf16[1152]{0:T(1024)(128)(2,1)}, u32[]{:S(2)}) copy-start(bf16[1152]{0:T(1024)(128)(2,1)} %param.39) | copy-start | bytes 6916
  9.4 87.1 %copy-start.7 = (bf16[1152]{0:T(1024)(128)(2,1)S(1)}, bf16[1152]{0:T(1024)(128)(2,1)}, u32[]{:S(2)}) copy-start(bf16[1152]{0:T(1024)(128)(2,1)} %param.41) | copy-start | bytes 6916
  9.4 87.1 %copy-start.13 = (s32[16,4]{0,1:T(4,128)S(1)}, s32[16,4]{0,1:T(4,128)}, u32[]{:S(2)}) copy-start(s32[16,4]{0,1:T(4,128)} %param.31) | copy-start | bytes 772
  9.4 87.3 %copy-start.10 = (bf16[576]{0:T(1024)(128)(2,1)S(1)}, bf16[576]{0:T(1024)(128)(2,1)}, u32[]{:S(2)}) copy-start(bf16[576]{0:T(1024)(128)(2,1)} %param.43) | copy-start | bytes 3460
  96.3 33.3 %collective-permute-start = (bf16[592,3456]{1,0:T(8,128)(2,1)}, bf16[592,3456]{1,0:T(8,128)(2,1)}, u32[]{:S(2)}, u32[]{:S(2)}) collective-permute-start(bf16[592,3456]{1,0:T(8,128)(2,1)} %copy.82), channel_id=1, source_target_pairs={{0,1},{1,0},{2,3},{3,2},{4,5},{5,4},{6,7},{7,6},{8,9},{9,8},{10,11... | collective-permute-start | bytes 12275720 | tf_op jit(solution)/shard_map/ppermute | solution.py:124
  98.8 13.3 %copy-start.14 = (bf16[72]{0:T(256)(128)(2,1)S(1)}, bf16[72]{0:T(256)(128)(2,1)}, u32[]{:S(2)}) copy-start(bf16[72]{0:T(256)(128)(2,1)} %param.47) | copy-start | bytes 436
  98.8 13.4 %copy-start.4 = (bf16[1152,72]{0,1:T(8,128)(2,1)S(1)}, bf16[1152,72]{0,1:T(8,128)(2,1)}, u32[]{:S(2)}) copy-start(bf16[1152,72]{0,1:T(8,128)(2,1)} %param.46) | copy-start | bytes 497668
  98.9 14.3 %copy-start.18 = (s32[1,4]{1,0:T(1,128)S(1)}, s32[1,4]{1,0:T(1,128)}, u32[]{:S(2)}) copy-start(s32[1,4]{1,0:T(1,128)} %param.33) | copy-start | bytes 52
  98.9 14.6 %copy-start.2 = (bf16[1,128,1152]{2,1,0:T(8,128)(2,1)S(1)}, bf16[1,128,1152]{2,1,0:T(8,128)(2,1)}, u32[]{:S(2)}) copy-start(bf16[1,128,1152]{2,1,0:T(8,128)(2,1)} %param.29) | copy-start | bytes 884740
  102.6 18.2 %all-to-all-start = ((bf16[16,4,576]{2,1,0:T(4,128)(2,1)}), bf16[16,4,576]{2,1,0:T(4,128)(2,1)S(1)}, u32[]{:S(2)}, u32[]{:S(2)}) async-start(bf16[16,4,576]{2,1,0:T(4,128)(2,1)} %reshape.206), calls=%async_computation | async-start | bytes 163840 | tf_op jit(solution)/shard_map/all_to_all | solution.py:102
  112.1 58.3 %all-gather.6.cloned.1.call-start = ((), (), s32[]{:S(2)}) async-start(), calls=%async_computation.6 | async-start | bytes 1566720 | tf_op jit(solution)/shard_map/all_gather | solution.py:121
  121.7 2.1 copy-start.1
  138.1 35.9 %all-to-all-start.1 = ((bf16[128,8,432]{0,2,1:T(8,128)(2,1)}), bf16[128,8,432]{0,2,1:T(8,128)(2,1)}, u32[]{:S(2)}, u32[]{:S(2)}) async-start(bf16[128,8,432]{0,2,1:T(8,128)(2,1)} %bitcast.96), calls=%async_computation.1 | async-start | bytes 1769472 | tf_op jit(solution)/shard_map/all_to_all | solution.py:143
  174.0 28.5 %collective-permute-start.1 = (bf16[592,1152]{1,0:T(8,128)(2,1)}, bf16[592,1152]{1,0:T(8,128)(2,1)}, u32[]{:S(2)}, u32[]{:S(2)}) collective-permute-start(bf16[592,1152]{1,0:T(8,128)(2,1)} %copy.89), channel_id=1, source_target_pairs={{0,1},{1,0},{2,3},{3,2},{4,5},{5,4},{6,7},{7,6},{8,9},{9,8},{10,11... | collective-permute-start | bytes 4091912 | tf_op jit(solution)/shard_map/ppermute | solution.py:124
  188.3 12.1 %all-to-all-start.2 = ((bf16[8,128,144]{1,2,0:T(8,128)(2,1)}), bf16[8,128,144]{1,2,0:T(8,128)(2,1)S(1)}, u32[]{:S(2)}, u32[]{:S(2)}) async-start(bf16[8,128,144]{1,2,0:T(8,128)(2,1)} %copy.87), calls=%async_computation.2 | async-start | bytes 589824 | tf_op jit(solution)/shard_map/all_to_all | solution.py:151
  192.6 39.5 %all-gather.8.cloned.1.call-start = ((), (), s32[]{:S(2)}) async-start(), calls=%async_computation.7 | async-start | bytes 2654208 | tf_op jit(solution)/shard_map/all_gather | solution.py:155
  200.4 2.1 copy-start.3
  204.6 2.5 copy-start.11
  207.0 70.6 %reduce-scatter.2.cloned.1.call-start = ((), (), s32[]{:S(2)}) async-start(), calls=%async_computation.8 | async-start | bytes 2654208 | tf_op jit(solution)/shard_map/reduce_scatter | solution.py:161
  240.0 0.7 copy-start.8
  240.0 0.7 copy-start.19
  240.0 39.3 %copy-start.5 = (bf16[1152,16]{0,1:T(8,128)(2,1)S(1)}, bf16[1152,16]{0,1:T(8,128)(2,1)}, u32[]{:S(2)}) copy-start(bf16[1152,16]{0,1:T(8,128)(2,1)} %param.52) | copy-start | bytes 110596
  240.7 44.0 %copy-start.15 = (f32[1,4]{1,0:T(1,128)S(1)}, f32[1,4]{1,0:T(1,128)}, u32[]{:S(2)}) copy-start(f32[1,4]{1,0:T(1,128)} %param.35) | copy-start | bytes 52
  240.7 44.0 %copy-start.16 = (f32[1,4]{1,0:T(1,128)S(1)}, f32[1,4]{1,0:T(1,128)}, u32[]{:S(2)}) copy-start(f32[1,4]{1,0:T(1,128)} %param.34) | copy-start | bytes 52
  240.7 44.0 %copy-start.17 = (f32[1,4]{1,0:T(1,128)S(1)}, f32[1,4]{1,0:T(1,128)}, u32[]{:S(2)}) copy-start(f32[1,4]{1,0:T(1,128)} %param.36) | copy-start | bytes 52
  240.7 47.8 %copy-start.9 = (f32[128,8]{0,1:T(8,128)S(1)}, f32[128,8]{0,1:T(8,128)}, u32[]{:S(2)}) copy-start(f32[128,8]{0,1:T(8,128)} %param.30) | copy-start | bytes 12292
  281.4 7.0 %all-to-all-start.3 = ((f32[1,128,16]{1,0,2:T(1,128)}), f32[1,128,16]{1,0,2:T(1,128)S(1)}, u32[]{:S(2)}, u32[]{:S(2)}) async-start(f32[1,128,16]{1,0,2:T(1,128)} %bitcast.21), calls=%async_computation.4 | async-start | bytes 16384 | tf_op jit(solution)/shard_map/all_to_all | solution.py:176
Sparse Core Ops, SparseCore 0:
  9.8 79.4 all-gather.3
  115.4 54.9 all-gather.5
  207.2 24.8 all-gather.7
  240.1 37.4 reduce-scatter.1
where the time goes:
time: 297 us; the launch traced here: 296 us
  waiting for transfers between devices  185 us (62%)
  matrix products  39.1 us (13%)
  local copies, waits for them, and re-layouts  24.1 us (8%)
  starting transfers between devices  21.3 us (7%)
  between operations  13.6 us (5%)
  other arithmetic  12 us (4%)
    all_gather x2, waiting for transfers between devices, split_gather(): lax.all_gather(jnp.concatenate([mine, bias_rows], axis=0), 'req', axis=1,...  106 us
    reduce_scatter x1, waiting for transfers between devices, shards(): lax.psum_scatter(jnp.dot(inner, down_weight, preferred_element_type=jnp.f...  37 us
    all_gather x1, waiting for transfers between devices, shards(): gathered = lax.all_gather(normed_mlp, 'mlp', axis=0, tiled=True)  25 us
    all_gather x2, local copies, waits for them, and re-layouts, split_gather(): lax.all_gather(jnp.concatenate([mine, bias_rows], axis=0), 'req', axis=1,...  10.6 us
    all_to_all x1, starting transfers between devices, shards(): lax.all_to_all(local_mod, 'req', split_axis=0, concat_axis=2, tiled=True)[0]  9.51 us
    sub x1, matrix products, attention(): expo = jnp.where(same, jnp.exp(masked - row_max), 0.0)  8.43 us
    dot_general x1, matrix products, shards(): jnp.dot(inner, down_weight, preferred_element_type=jnp.float32)  7.88 us
    all_to_all x1, waiting for transfers between devices, shards(): lax.all_to_all(local_mod, 'req', split_axis=0, concat_axis=2, tiled=True)[0]  6.92 us
  transfers between devices with their start and end apart: 10, of which 7 were waited for; matrix products, arithmetic and copies ran while one was open for 16% of the time, Pallas kernels for 0%

commit v1 on v0

--- a/solution.py
+++ b/solution.py
@@ -152,7 +152,9 @@
     projected = split_dot(attended, out_mine, out_other)
     mid_hidden = (rows.astype(jnp.float32) + gate_attn * projected).astype(jnp.bfloat16)
     normed_mlp = (layer_norm(mid_hidden) * (1.0 + scale_mlp) + shift_mlp).astype(jnp.bfloat16)
-    gathered = lax.all_gather(normed_mlp, "mlp", axis=0, tiled=True)
+    gathered = jnp.concatenate(
+        lax.all_to_all(jnp.stack([normed_mlp] * lax.axis_size("mlp")), "mlp", 0, 0), axis=0
+    )
     inner = jax.nn.gelu(
         jnp.dot(gathered, up_weight, preferred_element_type=jnp.float32)
         + up_bias.astype(jnp.float32),

time: 297 us -> 303 us (1.020)
  starting transfers between devices: 21.3 us -> 25.8 us
    all_to_all x0 -> x1, waiting for transfers between devices: none -> 29.9 us  [shards(): lax.all_to_all(jnp.stack([normed_mlp] * lax.axis_size('mlp')), 'mlp', 0, 0)]
    all_gather x1 -> x0, waiting for transfers between devices: 25 us -> none  [shards(): gathered = lax.all_gather(normed_mlp, 'mlp', axis=0, tiled=True)]
    all_to_all x0 -> x1, starting transfers between devices: none -> 4.5 us  [shards(): lax.all_to_all(jnp.stack([normed_mlp] * lax.axis_size('mlp')), 'mlp', 0, 0)]
    reduce_scatter x1, waiting for transfers between devices: 37 us -> 33.2 us  [shards(): lax.psum_scatter(jnp.dot(inner, down_weight, preferred_element_type=jnp.f...]
  transfers between devices with their start and end apart: 10 -> 10, of which waited for: 7 -> 7; matrix products, arithmetic and copies ran while one was open for 16% -> 15% of each run, Pallas kernels for 0% -> 0%
where the time goes in v1:
time: 303 us; the launch traced here: 302 us
  waiting for transfers between devices  187 us (62%)
  matrix products  39.1 us (13%)
  local copies, waits for them, and re-layouts  25.9 us (9%)
  starting transfers between devices  25.8 us (9%)
  between operations  13.6 us (4%)
  other arithmetic  11.2 us (4%)
    all_gather x2, waiting for transfers between devices, split_gather(): lax.all_gather(jnp.concatenate([mine, bias_rows], axis=0), 'req', axis=1,...  106 us
    reduce_scatter x1, waiting for transfers between devices, shards(): lax.psum_scatter(jnp.dot(inner, down_weight, preferred_element_type=jnp.f...  33.2 us
    all_to_all x1, waiting for transfers between devices, shards(): lax.all_to_all(jnp.stack([normed_mlp] * lax.axis_size('mlp')), 'mlp', 0, 0)  29.9 us
    all_gather x2, local copies, waits for them, and re-layouts, split_gather(): lax.all_gather(jnp.concatenate([mine, bias_rows], axis=0), 'req', axis=1,...  10.6 us
    all_to_all x1, starting transfers between devices, shards(): lax.all_to_all(local_mod, 'req', split_axis=0, concat_axis=2, tiled=True)[0]  9.51 us
    sub x1, matrix products, attention(): expo = jnp.where(same, jnp.exp(masked - row_max), 0.0)  8.44 us
    dot_general x1, matrix products, shards(): jnp.dot(inner, down_weight, preferred_element_type=jnp.float32)  7.88 us
    all_to_all x1, waiting for transfers between devices, shards(): lax.all_to_all(local_mod, 'req', split_axis=0, concat_axis=2, tiled=True)[0]  6.91 us
  transfers between devices with their start and end apart: 10, of which 7 were waited for; matrix products, arithmetic and copies ran while one was open for 15% of the time, Pallas kernels for 0%

profile of v1, /device:TPU:8, one launch (start us, length us, event | category | flops | bytes accessed | tf_op | source)
XLA Modules:
  0.0 302.2 jit_solution(4490757149535602058)
XLA Ops:
  9.5 79.9 %all-gather.3.cloned.1.call-done = bf16[592,3456]{0,1:T(8,128)(2,1)} async-done(((bf16[592,216]{0,1:T(8,128)(2,1)}), bf16[592,3456]{0,1:T(8,128)(2,1)}) %all-gather.3.cloned.1.call-update) | async-done | bytes 4091920 | tf_op jit(solution)/shard_map/all_gather | solution.py:121
  89.3 7.0 %copy.82 = bf16[592,3456]{1,0:T(8,128)(2,1)} copy(bf16[592,3456]{0,1:T(8,128)(2,1)} %all-gather.3.cloned.1.call-done) | data formatting | bytes 8183808 | tf_op jit(solution)/shard_map/all_gather | solution.py:121
  97.0 1.8 convolution_add_fusion.3
  98.9 3.0 %fusion.37 = bf16[64,576]{1,0:T(8,128)(2,1)S(1)} fusion(bf16[1152,576]{0,1:T(8,128)(2,1)} %param.42, f32[64,1152]{1,0:T(8,128)S(1)} %convolution_add_fusion.3, bf16[1001,1152]{1,0:T(8,128)(2,1)} %param.37, s32[64]{0:T(128)S(1)} %select_n.45, f32[576]{0:T(1024)S(1)} %convert_element_type.98), kind=kOutput, calls=%fused_computation.43 | convolution fusion | flops 233118272 | bytes 4004608 | tf_op jit(solution)/shard_map/dot_general | solution.py:98
  102.6 9.5 %all-to-all-start = ((bf16[16,4,576]{2,1,0:T(4,128)(2,1)}), bf16[16,4,576]{2,1,0:T(4,128)(2,1)S(1)}, u32[]{:S(2)}, u32[]{:S(2)}) async-start(bf16[16,4,576]{2,1,0:T(4,128)(2,1)} %reshape.211), calls=%async_computation | async-start | bytes 163840 | tf_op jit(solution)/shard_map/all_to_all | solution.py:102
  113.9 6.9 %all-to-all-done = bf16[16,4,576]{2,1,0:T(4,128)(2,1)S(1)} async-done(((bf16[16,4,576]{2,1,0:T(4,128)(2,1)}), bf16[16,4,576]{2,1,0:T(4,128)(2,1)S(1)}, u32[]{:S(2)}, u32[]{:S(2)}) %all-to-all-start) | async-done | bytes 73760 | tf_op jit(solution)/shard_map/all_to_all | solution.py:102
  121.8 2.1 copy-done.1
  124.2 1.8 convert_reduce_fusion
  126.0 3.7 %fusion.4 = f32[128,3456]{1,0:T(8,128)S(1)} fusion(bf16[592,3456]{0,1:T(8,128)(2,1)} %all-gather.3.cloned.1.call-done, bf16[128,1152]{1,0:T(8,128)(2,1)S(1)} %fusion.46, s32[]{:T(128)S(6)} %select_n.47), kind=kOutput, calls=%fused_computation.7 | convolution fusion | flops 509607936 | bytes 6025220 | tf_op jit(solution)/shard_map/dot_general | solution.py:130
  129.7 4.0 %fusion.3 = bf16[128,3456]{1,0:T(8,128)(2,1)} fusion(f32[128,3456]{1,0:T(8,128)S(1)} %fusion.4, bf16[592,3456]{1,0:T(8,128)(2,1)} %collective-permute-done, f32[3456]{0:T(1024)S(1)} %convert_reduce_fusion, bf16[128,1152]{1,0:T(8,128)(2,1)S(1)} %fusion.46, s32[]{:T(128)S(6)} %select_n.48), kind=kOutput, calls=%fused_computation.6 | convolution fusion | flops 510935040 | bytes 6815748 | tf_op jit(solution)/shard_map/dot_general | solution.py:131
  133.8 2.2 copy.83
  136.0 2.1 copy.84
  138.1 4.2 %all-to-all-start.1 = ((bf16[128,8,432]{0,2,1:T(8,128)(2,1)}), bf16[128,8,432]{0,2,1:T(8,128)(2,1)}, u32[]{:S(2)}, u32[]{:S(2)}) async-start(bf16[128,8,432]{0,2,1:T(8,128)(2,1)} %bitcast.97), calls=%async_computation.1 | async-start | bytes 1769472 | tf_op jit(solution)/shard_map/all_to_all | solution.py:143
  142.4 1.7 broadcast_compare_fusion
  144.0 26.4 %all-gather.5.cloned.1.call-done = bf16[592,1152]{0,1:T(8,128)(2,1)} async-done(((bf16[592,72]{0,1:T(8,128)(2,1)}), bf16[592,1152]{0,1:T(8,128)(2,1)}) %all-gather.5.cloned.1.call-update) | async-done | bytes 1363984 | tf_op jit(solution)/shard_map/all_gather | solution.py:121
  170.4 3.6 %copy.89 = bf16[592,1152]{1,0:T(8,128)(2,1)} copy(bf16[592,1152]{0,1:T(8,128)(2,1)} %all-gather.5.cloned.1.call-done) | data formatting | bytes 2727936 | tf_op jit(solution)/shard_map/all_gather | solution.py:121
  176.1 8.4 %fusion.99 = (f32[2,1024]{1,0:T(2,128)S(1)}, bf16[2,1024,1024]{1,2,0:T(8,128)(2,1)}) fusion(pred[1024,1024]{0,1:T(8,128)(4,1)} %broadcast_compare_fusion, bf16[1024,2,72]{0,2,1:T(8,128)(2,1)} %bitcast.105, bf16[1024,2,72]{0,2,1:T(8,128)(2,1)S(1)} %bitcast.104), kind=kOutput, calls=%fused_computation.135 | convolution fusion | flops 314573824 | bytes 5840896 | tf_op jit(solution)/shard_map/sub | solution.py:39
  184.5 3.0 %fusion.34 = bf16[1024,2,72]{0,2,1:T(8,128)(2,1)S(1)} fusion(bf16[1024,2,72]{0,2,1:T(8,128)(2,1)S(1)} %bitcast.103, bf16[2,1024,1024]{1,2,0:T(8,128)(2,1)} %get-tuple-element.40, f32[1024,2]{0,1:T(2,128)S(1)} %bitcast.114), kind=kOutput, calls=%fused_computation.41 | convolution fusion | flops 302284800 | bytes 4792320 | tf_op jit(solution)/shard_map/hqk,khd->qhd/dot_general | solution.py:42
  188.4 4.2 %all-to-all-start.2 = ((bf16[8,128,144]{1,2,0:T(8,128)(2,1)}), bf16[8,128,144]{1,2,0:T(8,128)(2,1)S(1)}, u32[]{:S(2)}, u32[]{:S(2)}) async-start(bf16[8,128,144]{1,2,0:T(8,128)(2,1)} %copy.87), calls=%async_computation.2 | async-start | bytes 589824 | tf_op jit(solution)/shard_map/all_to_all | solution.py:151
  193.8 6.6 %all-to-all-done.2 = bf16[8,128,144]{1,2,0:T(8,128)(2,1)S(1)} async-done(((bf16[8,128,144]{1,2,0:T(8,128)(2,1)}), bf16[8,128,144]{1,2,0:T(8,128)(2,1)S(1)}, u32[]{:S(2)}, u32[]{:S(2)}) %all-to-all-start.2) | async-done | bytes 294944 | tf_op jit(solution)/shard_map/all_to_all | solution.py:151
  200.5 2.1 fusion.25
  202.6 2.1 fusion.100
  204.9 1.4 fusion.49
  206.3 1.8 stack.2
  208.1 4.5 %all-to-all-start.3 = ((bf16[8,128,1152]{2,1,0:T(8,128)(2,1)}), bf16[8,128,1152]{2,1,0:T(8,128)(2,1)}, u32[]{:S(2)}, u32[]{:S(2)}) async-start(bf16[8,128,1152]{2,1,0:T(8,128)(2,1)} %stack.2), calls=%async_computation.3 | async-start | bytes 4718592 | tf_op jit(solution)/shard_map/all_to_all | solution.py:156
  212.7 29.9 %all-to-all-done.3 = bf16[8,128,1152]{2,1,0:T(8,128)(2,1)} async-done(((bf16[8,128,1152]{2,1,0:T(8,128)(2,1)}), bf16[8,128,1152]{2,1,0:T(8,128)(2,1)}, u32[]{:S(2)}, u32[]{:S(2)}) %all-to-all-start.3) | async-done | bytes 2359328 | tf_op jit(solution)/shard_map/all_to_all | solution.py:156
  242.6 7.9 %convolution_convert_fusion = bf16[1024,1152]{1,0:T(8,128)(2,1)} fusion(bf16[576,1152]{1,0:T(8,128)(2,1)} %param.50, bf16[1024,1152]{1,0:T(8,128)(2,1)} %bitcast.20, bf16[1152,576]{0,1:T(8,128)(2,1)} %param.48, f32[576]{0:T(1024)S(1)} %convert_element_type.107), kind=kOutput, calls=%fused_computation.15 | convolution fusion | flops 2724986880 | bytes 7375104 | tf_op jit(solution)/shard_map/dot_general | solution.py:164
  251.2 33.2 %reduce-scatter.2.cloned.1.call-done = bf16[128,1152]{1,0:T(8,128)(2,1)} async-done(((bf16[1024,1152]{1,0:T(8,128)(2,1)}), bf16[128,1152]{1,0:T(8,128)(2,1)}) %reduce-scatter.2.cloned.1.call-update) | async-done | bytes 294928 | tf_op jit(solution)/shard_map/reduce_scatter | solution.py:163
  284.3 1.3 fusion.96
  285.9 2.2 convolution_add_fusion.6
  288.1 3.2 %all-to-all-start.4 = ((f32[1,128,16]{1,0,2:T(1,128)}), f32[1,128,16]{1,0,2:T(1,128)S(1)}, u32[]{:S(2)}, u32[]{:S(2)}) async-start(f32[1,128,16]{1,0,2:T(1,128)} %bitcast.22), calls=%async_computation.5 | async-start | bytes 16384 | tf_op jit(solution)/shard_map/all_to_all | solution.py:178
  291.4 3.7 %all-to-all-done.4 = f32[1,128,16]{1,0,2:T(1,128)S(1)} async-done(((f32[1,128,16]{1,0,2:T(1,128)}), f32[1,128,16]{1,0,2:T(1,128)S(1)}, u32[]{:S(2)}, u32[]{:S(2)}) %all-to-all-start.4) | async-done | bytes 8224 | tf_op jit(solution)/shard_map/all_to_all | solution.py:178
  (95 shorter events, 13.0 us)
Async XLA Ops:
  6.5 90.5 %copy-start = (bf16[1152,1152]{1,0:T(8,128)(2,1)S(1)}, bf16[1152,1152]{1,0:T(8,128)(2,1)}, u32[]{:S(2)}) copy-start(bf16[1152,1152]{1,0:T(8,128)(2,1)} %param.40) | copy-start | bytes 7962628
  6.5 82.8 %all-gather.3.cloned.1.call-start = ((), (), s32[]{:S(2)}) async-start(), calls=%async_computation.6 | async-start | bytes 4700160 | tf_op jit(solution)/shard_map/all_gather | solution.py:121
  9.4 87.0 %copy-start.12 = (s32[16,4]{0,1:T(4,128)S(1)}, s32[16,4]{0,1:T(4,128)}, u32[]{:S(2)}) copy-start(s32[16,4]{0,1:T(4,128)} %param.32) | copy-start | bytes 772
  9.4 87.1 %copy-start.6 = (bf16[1152]{0:T(1024)(128)(2,1)S(1)}, bf16[1152]{0:T(1024)(128)(2,1)}, u32[]{:S(2)}) copy-start(bf16[1152]{0:T(1024)(128)(2,1)} %param.39) | copy-start | bytes 6916
  9.4 87.1 %copy-start.7 = (bf16[1152]{0:T(1024)(128)(2,1)S(1)}, bf16[1152]{0:T(1024)(128)(2,1)}, u32[]{:S(2)}) copy-start(bf16[1152]{0:T(1024)(128)(2,1)} %param.41) | copy-start | bytes 6916
  9.4 87.2 %copy-start.13 = (s32[16,4]{0,1:T(4,128)S(1)}, s32[16,4]{0,1:T(4,128)}, u32[]{:S(2)}) copy-start(s32[16,4]{0,1:T(4,128)} %param.31) | copy-start | bytes 772
  9.4 87.3 %copy-start.10 = (bf16[576]{0:T(1024)(128)(2,1)S(1)}, bf16[576]{0:T(1024)(128)(2,1)}, u32[]{:S(2)}) copy-start(bf16[576]{0:T(1024)(128)(2,1)} %param.43) | copy-start | bytes 3460
  96.4 33.3 %collective-permute-start = (bf16[592,3456]{1,0:T(8,128)(2,1)}, bf16[592,3456]{1,0:T(8,128)(2,1)}, u32[]{:S(2)}, u32[]{:S(2)}) collective-permute-start(bf16[592,3456]{1,0:T(8,128)(2,1)} %copy.82), channel_id=1, source_target_pairs={{0,1},{1,0},{2,3},{3,2},{4,5},{5,4},{6,7},{7,6},{8,9},{9,8},{10,11... | collective-permute-start | bytes 12275720 | tf_op jit(solution)/shard_map/ppermute | solution.py:124
  98.8 13.3 %copy-start.14 = (bf16[72]{0:T(256)(128)(2,1)S(1)}, bf16[72]{0:T(256)(128)(2,1)}, u32[]{:S(2)}) copy-start(bf16[72]{0:T(256)(128)(2,1)} %param.47) | copy-start | bytes 436
  98.9 13.4 %copy-start.4 = (bf16[1152,72]{0,1:T(8,128)(2,1)S(1)}, bf16[1152,72]{0,1:T(8,128)(2,1)}, u32[]{:S(2)}) copy-start(bf16[1152,72]{0,1:T(8,128)(2,1)} %param.46) | copy-start | bytes 497668
  98.9 14.3 %copy-start.18 = (s32[1,4]{1,0:T(1,128)S(1)}, s32[1,4]{1,0:T(1,128)}, u32[]{:S(2)}) copy-start(s32[1,4]{1,0:T(1,128)} %param.33) | copy-start | bytes 52
  98.9 14.6 %copy-start.2 = (bf16[1,128,1152]{2,1,0:T(8,128)(2,1)S(1)}, bf16[1,128,1152]{2,1,0:T(8,128)(2,1)}, u32[]{:S(2)}) copy-start(bf16[1,128,1152]{2,1,0:T(8,128)(2,1)} %param.29) | copy-start | bytes 884740
  102.6 18.2 %all-to-all-start = ((bf16[16,4,576]{2,1,0:T(4,128)(2,1)}), bf16[16,4,576]{2,1,0:T(4,128)(2,1)S(1)}, u32[]{:S(2)}, u32[]{:S(2)}) async-start(bf16[16,4,576]{2,1,0:T(4,128)(2,1)} %reshape.211), calls=%async_computation | async-start | bytes 163840 | tf_op jit(solution)/shard_map/all_to_all | solution.py:102
  112.1 58.3 %all-gather.5.cloned.1.call-start = ((), (), s32[]{:S(2)}) async-start(), calls=%async_computation.7 | async-start | bytes 1566720 | tf_op jit(solution)/shard_map/all_gather | solution.py:121
  121.8 2.1 copy-start.1
  138.1 35.9 %all-to-all-start.1 = ((bf16[128,8,432]{0,2,1:T(8,128)(2,1)}), bf16[128,8,432]{0,2,1:T(8,128)(2,1)}, u32[]{:S(2)}, u32[]{:S(2)}) async-start(bf16[128,8,432]{0,2,1:T(8,128)(2,1)} %bitcast.97), calls=%async_computation.1 | async-start | bytes 1769472 | tf_op jit(solution)/shard_map/all_to_all | solution.py:143
  174.0 28.5 %collective-permute-start.1 = (bf16[592,1152]{1,0:T(8,128)(2,1)}, bf16[592,1152]{1,0:T(8,128)(2,1)}, u32[]{:S(2)}, u32[]{:S(2)}) collective-permute-start(bf16[592,1152]{1,0:T(8,128)(2,1)} %copy.89), channel_id=1, source_target_pairs={{0,1},{1,0},{2,3},{3,2},{4,5},{5,4},{6,7},{7,6},{8,9},{9,8},{10,11... | collective-permute-start | bytes 4091912 | tf_op jit(solution)/shard_map/ppermute | solution.py:124
  188.4 12.1 %all-to-all-start.2 = ((bf16[8,128,144]{1,2,0:T(8,128)(2,1)}), bf16[8,128,144]{1,2,0:T(8,128)(2,1)S(1)}, u32[]{:S(2)}, u32[]{:S(2)}) async-start(bf16[8,128,144]{1,2,0:T(8,128)(2,1)} %copy.87), calls=%async_computation.2 | async-start | bytes 589824 | tf_op jit(solution)/shard_map/all_to_all | solution.py:151
  200.5 2.1 copy-start.3
  208.1 4.6 %copy-start.11 = (bf16[576]{0:T(1024)(128)(2,1)S(1)}, bf16[576]{0:T(1024)(128)(2,1)}, u32[]{:S(2)}) copy-start(bf16[576]{0:T(1024)(128)(2,1)} %param.49) | copy-start | bytes 3460
  208.1 34.5 %all-to-all-start.3 = ((bf16[8,128,1152]{2,1,0:T(8,128)(2,1)}), bf16[8,128,1152]{2,1,0:T(8,128)(2,1)}, u32[]{:S(2)}, u32[]{:S(2)}) async-start(bf16[8,128,1152]{2,1,0:T(8,128)(2,1)} %stack.2), calls=%async_computation.3 | async-start | bytes 4718592 | tf_op jit(solution)/shard_map/all_to_all | solution.py:156
  212.6 71.8 %reduce-scatter.2.cloned.1.call-start = ((), (), s32[]{:S(2)}) async-start(), calls=%async_computation.8 | async-start | bytes 2654208 | tf_op jit(solution)/shard_map/reduce_scatter | solution.py:163
  250.5 0.7 copy-start.8
  250.5 0.7 copy-start.19
  250.5 35.5 %copy-start.5 = (bf16[1152,16]{0,1:T(8,128)(2,1)S(1)}, bf16[1152,16]{0,1:T(8,128)(2,1)}, u32[]{:S(2)}) copy-start(bf16[1152,16]{0,1:T(8,128)(2,1)} %param.52) | copy-start | bytes 110596
  251.1 40.2 %copy-start.15 = (f32[1,4]{1,0:T(1,128)S(1)}, f32[1,4]{1,0:T(1,128)}, u32[]{:S(2)}) copy-start(f32[1,4]{1,0:T(1,128)} %param.35) | copy-start | bytes 52
  251.1 40.2 %copy-start.16 = (f32[1,4]{1,0:T(1,128)S(1)}, f32[1,4]{1,0:T(1,128)}, u32[]{:S(2)}) copy-start(f32[1,4]{1,0:T(1,128)} %param.34) | copy-start | bytes 52
  251.1 40.2 %copy-start.17 = (f32[1,4]{1,0:T(1,128)S(1)}, f32[1,4]{1,0:T(1,128)}, u32[]{:S(2)}) copy-start(f32[1,4]{1,0:T(1,128)} %param.36) | copy-start | bytes 52
  251.2 44.0 %copy-start.9 = (f32[128,8]{0,1:T(8,128)S(1)}, f32[128,8]{0,1:T(8,128)}, u32[]{:S(2)}) copy-start(f32[128,8]{0,1:T(8,128)} %param.30) | copy-start | bytes 12292
  288.1 7.0 %all-to-all-start.4 = ((f32[1,128,16]{1,0,2:T(1,128)}), f32[1,128,16]{1,0,2:T(1,128)S(1)}, u32[]{:S(2)}, u32[]{:S(2)}) async-start(f32[1,128,16]{1,0,2:T(1,128)} %bitcast.22), calls=%async_computation.5 | async-start | bytes 16384 | tf_op jit(solution)/shard_map/all_to_all | solution.py:178
Sparse Core Ops, SparseCore 0:
  9.8 79.4 all-gather.2
  115.4 54.9 all-gather.4
  250.6 33.6 reduce-scatter.1
